TPU v7x, 32 devices: a whole 2x2x4 slice. The times are simulated.
32 devices in a mesh: section: 4 (over x, core), expert: 8 (over z, y).
Axes of the slice: x: 2, y: 2, z: 4, core: 2. Of those that a mesh axis runs over, the one named last changes fastest.
Arguments:
- layer_inputs: bfloat16 [4, 8, 128, 2048], P('section', None, 'expert'), may hold values from -6 to 6
- top_grad: bfloat16 [8, 128, 2048], P('section', 'expert'), may hold values from -6 to 6
- expert_ids: int32 [4, 8, 128, 4], P('section', None, 'expert'), may hold values from 0 to 7, all different within a row; in each aligned block of 16 rows (0 to 15, 16 to 31, ..., all dimensions but the last counted through in order) at most 9 rows name the same one
- router: bfloat16 [4, 2048, 8], P('section'), may hold values from -0.125 to 0.125
- norm_gain: bfloat16 [4, 2048], P('section'), may hold values from 0.099609375 to 1.8984375
- w_gate: bfloat16 [4, 8, 2048, 1024], P('section', 'expert'), may hold values from -0.125 to 0.125
- w_up: bfloat16 [4, 8, 2048, 1024], P('section', 'expert'), may hold values from -0.125 to 0.125
- w_down: bfloat16 [4, 8, 1024, 2048], P('section', 'expert'), may hold values from -0.1875 to 0.1875
Outputs:
- input_grads: bfloat16 [4, 8, 128, 2048], P('section', None, 'expert')
Inputs may be any that keep to these rules, and one draw needn't show every extreme that they name: `expert_ids`: each token names 4 different experts. Among the 16 tokens of one device in one micro-batch of one layer, no expert is named by more than 9 of them, and in some of these blocks one expert is named by exactly 9.
All inputs are finite; a program needn't handle non-finite values.
Results may differ from a plain program's by a relative error of at most 0.015.
Values may be sent and summed in bfloat16 or wider, within the bound.
No kernel may reach another device: no remote copies, remote signals or barrier semaphores. Data moves between devices by JAX's collectives and lax.ppermute only.
A program may use at most 128 MiB of HBM per device.

v0:
```python
import jax
import jax.numpy as jnp
from jax import lax
from jax.sharding import PartitionSpec as P


def shifted(shard, axis, by):
    devices = lax.axis_size(axis)
    pairs = [(i, i + by) for i in range(devices) if 0 <= i + by < devices]
    return lax.ppermute(shard, axis, pairs)


def prepare(x_rows, gain):
    x_float = x_rows.astype(jnp.float32)
    inverse = lax.rsqrt(jnp.mean(x_float * x_float, axis=-1, keepdims=True) + 1e-05)
    normed = (x_float * inverse * gain).astype(jnp.bfloat16)
    return (x_float, inverse, normed)


def expert_rows(normed_rows, grad_rows, gate_w, up_w, down_w):
    gate = jnp.dot(normed_rows, gate_w, preferred_element_type=jnp.float32)
    up_rows = jnp.dot(normed_rows, up_w, preferred_element_type=jnp.float32)
    squash = jax.nn.sigmoid(gate)
    active = gate * squash
    hidden = (active * up_rows).astype(jnp.bfloat16)
    output = jnp.dot(hidden, down_w, preferred_element_type=jnp.float32)
    dprob = jnp.sum(output * grad_rows.astype(jnp.float32), axis=-1)
    dhidden = lax.dot_general(
        grad_rows, down_w, (((1,), (1,)), ((), ())), preferred_element_type=jnp.float32
    )
    dgate = (dhidden * up_rows * squash * (1.0 + gate * (1.0 - squash))).astype(jnp.bfloat16)
    dup = (dhidden * active).astype(jnp.bfloat16)
    returned = lax.dot_general(
        dgate, gate_w, (((1,), (1,)), ((), ())), preferred_element_type=jnp.float32
    )
    returned = returned + lax.dot_general(
        dup, up_w, (((1,), (1,)), ((), ())), preferred_element_type=jnp.float32
    )
    return (returned.astype(jnp.bfloat16), dprob)


def finish(x_float, inverse, normed, gain, router_layer, ids, grad_in, pair_back, pair_prob):
    logits = jnp.dot(normed, router_layer, preferred_element_type=jnp.float32)
    raised = jnp.exp(logits)
    probs = raised / jnp.sum(raised, axis=-1, keepdims=True)
    choose = (ids[..., None] == jnp.arange(router_layer.shape[1], dtype=jnp.int32)).astype(
        jnp.float32
    )
    picked = jnp.sum(probs[..., None, :] * choose, axis=-1)
    dfull = jnp.sum(pair_prob[..., None] * choose, axis=-2)
    dlogit = probs * (dfull - jnp.sum(probs * dfull, axis=-1, keepdims=True))
    router_term = jnp.dot(
        dlogit, router_layer.astype(jnp.float32).T, precision=lax.Precision.HIGHEST
    )
    dnormed = jnp.sum(picked[..., None] * pair_back, axis=-2) + router_term
    scaled = gain * dnormed
    inner = jnp.mean(x_float * scaled, axis=-1, keepdims=True)
    result = (
        grad_in.astype(jnp.float32)
        + inverse * scaled
        - x_float * inverse * inverse * inverse * inner
    )
    return result.astype(jnp.bfloat16)


def selection(ids, experts, capacity):
    pair_ids = ids.reshape(-1)
    onehot = (pair_ids[:, None] == jnp.arange(experts, dtype=jnp.int32)[None, :]).astype(jnp.int32)
    ranks = jnp.sum(onehot * (jnp.cumsum(onehot, axis=0) - 1), axis=1)
    target = pair_ids * capacity + ranks
    return (target[:, None] == jnp.arange(experts * capacity, dtype=jnp.int32)[None, :]).astype(
        jnp.bfloat16
    )


def pack_rows(select, rows, per_token):
    repeated = jnp.repeat(rows, per_token, axis=0)
    packed = lax.dot_general(
        select, repeated, (((0,), (0,)), ((), ())), preferred_element_type=jnp.float32
    )
    return packed.astype(jnp.bfloat16)


def pick_micro(values, index):
    return lax.dynamic_index_in_dim(values, index, 0, False)


def shards(layer_inputs, top_grad, expert_ids, router, norm_gain, w_gate, w_up, w_down):
    segments = lax.axis_size("section")
    experts = lax.axis_size("expert")
    segment_index = lax.axis_index("section")
    micro = layer_inputs.shape[1]
    tok_rows = layer_inputs.shape[2]
    width = layer_inputs.shape[3]
    per_token = expert_ids.shape[3]
    capacity = min(tok_rows, per_token * tok_rows // experts + max(1, tok_rows // 16))
    slots = experts * capacity
    gain = norm_gain[0].astype(jnp.float32)
    router_layer = router[0]
    gate_layer = w_gate[0, 0]
    up_layer = w_up[0, 0]
    down_layer = w_down[0, 0]
    ids_layer = expert_ids[0]
    x_layer = layer_inputs[0]
    top_full = lax.all_gather(top_grad, "section", axis=0, tiled=True)

    def advance(step, carry):
        previous, collected = carry
        arrived = shifted(previous, "section", -1)
        position = step - (segments - 1 - segment_index)
        working = jnp.logical_and(position >= 0, position < micro)
        chosen = jnp.clip(position, 0, micro - 1)
        grad_in = jnp.where(segment_index == segments - 1, pick_micro(top_full, chosen), arrived)
        ids_now = pick_micro(ids_layer, chosen)
        select = selection(ids_now, experts, capacity)
        x_float, inverse, normed = prepare(pick_micro(x_layer, chosen), gain)
        sent_normed = pack_rows(select, normed, per_token).reshape(experts, capacity, width)
        sent_grad = pack_rows(select, grad_in, per_token).reshape(experts, capacity, width)
        got_normed, got_grad = (
            lax.all_to_all(sent_normed, "expert", split_axis=0, concat_axis=0, tiled=True),
            lax.all_to_all(sent_grad, "expert", split_axis=0, concat_axis=0, tiled=True),
        )
        rows_normed = got_normed.reshape(slots, width)
        rows_grad = got_grad.reshape(slots, width)

        def run_expert(operands):
            return expert_rows(operands[0], operands[1], gate_layer, up_layer, down_layer)

        def skip_expert(operands):
            return (jnp.zeros((slots, width), jnp.bfloat16), jnp.zeros((slots,), jnp.float32))

        returned, dprob = lax.cond(working, run_expert, skip_expert, (rows_normed, rows_grad))
        back_home, prob_home = (
            lax.all_to_all(
                returned.reshape(experts, capacity, width),
                "expert",
                split_axis=0,
                concat_axis=0,
                tiled=True,
            ),
            lax.all_to_all(
                dprob.reshape(experts, capacity).astype(jnp.bfloat16),
                "expert",
                split_axis=0,
                concat_axis=0,
                tiled=True,
            ).astype(jnp.float32),
        )
        pair_back = lax.dot_general(
            select,
            back_home.reshape(slots, width),
            (((1,), (0,)), ((), ())),
            preferred_element_type=jnp.float32,
        )
        pair_back = pair_back.reshape(tok_rows, per_token, width)
        pair_prob = jnp.dot(
            select.astype(jnp.float32), prob_home.reshape(slots), precision=lax.Precision.HIGHEST
        )
        pair_prob = pair_prob.reshape(tok_rows, per_token)
        result = finish(
            x_float, inverse, normed, gain, router_layer, ids_now, grad_in, pair_back, pair_prob
        )
        retained = pick_micro(collected, chosen)
        collected = lax.dynamic_update_index_in_dim(
            collected, jnp.where(working, result, retained), chosen, 0
        )
        return (result, collected)

    start = (
        jnp.zeros((tok_rows, width), jnp.bfloat16),
        jnp.zeros((micro, tok_rows, width), jnp.bfloat16),
    )
    final_grad, collected = lax.fori_loop(0, micro + segments - 1, advance, start)
    return collected.reshape(1, micro, tok_rows, width)


def solution(mesh):
    placed = (
        P("section", None, "expert", None),
        P("section", "expert", None),
        P("section", None, "expert", None),
        P("section", None, None),
        P("section", None),
        P("section", "expert", None, None),
        P("section", "expert", None, None),
        P("section", "expert", None, None),
    )
    return jax.shard_map(
        shards,
        mesh=mesh,
        in_specs=placed,
        out_specs=P("section", None, "expert", None),
        check_vma=False,
    )
```

profile of v0, /device:TPU:2, one launch (start us, length us, event | category | flops | bytes accessed | tf_op | source)
XLA Modules:
  0.0 932.1 jit_solution(10642153080023947241)
XLA Ops:
  9.2 922.1 %while.18 = (s32[]{:T(128)}, bf16[16,2048]{1,0:T(8,128)(2,1)S(1)}, bf16[8,16,2048]{2,1,0:T(8,128)(2,1)S(1)}, pred[]{:T(512)}, s32[]{:T(128)}, /*index=5*/bf16[8,...) while((s32[]{:T(128)}, bf16[16,2048]{1,0:T(8,128)(2,1)S(1)}, ...), condition=%wide.region_13.14_spmd.clone, body=%wide.region_0.13_spmd.clone.sunk | while | flops 1876001664 | bytes 93928576 | solution.py:173
  40.5 14.4 %all-to-all-done = bf16[8,9,2048]{2,1,0:T(8,128)(2,1)S(1)} async-done(((bf16[8,9,2048]{2,1,0:T(8,128)(2,1)}), bf16[8,9,2048]{2,1,0:T(8,128)(2,1)S(1)}, u32[]{:S(2)}, u32[]{:S(2)}) %all-to-all-start) | async-done | bytes 294944 | tf_op jit(solution)/shard_map/while/body/eval_jaxpr/all_to_all | solution.py:121
  120.1 14.1 %conditional.3 = (bf16[72,2048]{1,0:T(8,128)(2,1)S(1)}, bf16[72]{0:T(256)(128)(2,1)S(1)}) conditional(s32[]{:T(128)} %convert_element_type.180, () %tuple.64, (bf16[8,9,2048]{2,1,0:T(8,128)(2,1)S(1)}, bf16[1024,2048]{1,0:T(8,128)(2,1)}, bf16[8,9,2048]{2,1,0:T(8,128)(2,1)S(1)}, bf16[2048,1024]{1,0:T(8,128)(2,1)}, bf16[2048,1024]{1,0:T(8,128)(2,1)}) %tuple.65), branch_computations={%region_6.6_spmd, %region_7.8_spmd} | conditional | flops 1814298624 | bytes 82280696 | solution.py:132
  151.3 14.9 %all-to-all-done.2 = bf16[8,9,2048]{2,1,0:T(8,128)(2,1)S(1)} async-done(((bf16[8,9,2048]{2,1,0:T(8,128)(2,1)}), bf16[8,9,2048]{2,1,0:T(8,128)(2,1)S(1)}, u32[]{:S(2)}, u32[]{:S(2)}) %all-to-all-start.2) | async-done | bytes 294944 | tf_op jit(solution)/shard_map/while/body/eval_jaxpr/all_to_all | solution.py:134
  180.9 13.7 %all-to-all-done.1 = bf16[8,9,2048]{2,1,0:T(8,128)(2,1)S(1)} async-done(((bf16[8,9,2048]{2,1,0:T(8,128)(2,1)}), bf16[8,9,2048]{2,1,0:T(8,128)(2,1)S(1)}, u32[]{:S(2)}, u32[]{:S(2)}) %all-to-all-start.1) | async-done | bytes 294944 | tf_op jit(solution)/shard_map/while/body/eval_jaxpr/all_to_all | solution.py:120
  198.4 14.5 %all-to-all-done = bf16[8,9,2048]{2,1,0:T(8,128)(2,1)S(1)} async-done(((bf16[8,9,2048]{2,1,0:T(8,128)(2,1)}), bf16[8,9,2048]{2,1,0:T(8,128)(2,1)S(1)}, u32[]{:S(2)}, u32[]{:S(2)}) %all-to-all-start) | async-done | bytes 294944 | tf_op jit(solution)/shard_map/while/body/eval_jaxpr/all_to_all | solution.py:121
  212.9 14.1 %conditional.3 = (bf16[72,2048]{1,0:T(8,128)(2,1)S(1)}, bf16[72]{0:T(256)(128)(2,1)S(1)}) conditional(s32[]{:T(128)} %convert_element_type.180, () %tuple.64, (bf16[8,9,2048]{2,1,0:T(8,128)(2,1)S(1)}, bf16[1024,2048]{1,0:T(8,128)(2,1)}, bf16[8,9,2048]{2,1,0:T(8,128)(2,1)S(1)}, bf16[2048,1024]{1,0:T(8,128)(2,1)}, bf16[2048,1024]{1,0:T(8,128)(2,1)}) %tuple.65), branch_computations={%region_6.6_spmd, %region_7.8_spmd} | conditional | flops 1814298624 | bytes 82280696 | solution.py:132
  269.0 13.7 %all-to-all-done.1 = bf16[8,9,2048]{2,1,0:T(8,128)(2,1)S(1)} async-done(((bf16[8,9,2048]{2,1,0:T(8,128)(2,1)}), bf16[8,9,2048]{2,1,0:T(8,128)(2,1)S(1)}, u32[]{:S(2)}, u32[]{:S(2)}) %all-to-all-start.1) | async-done | bytes 294944 | tf_op jit(solution)/shard_map/while/body/eval_jaxpr/all_to_all | solution.py:120
  286.6 14.5 %all-to-all-done = bf16[8,9,2048]{2,1,0:T(8,128)(2,1)S(1)} async-done(((bf16[8,9,2048]{2,1,0:T(8,128)(2,1)}), bf16[8,9,2048]{2,1,0:T(8,128)(2,1)S(1)}, u32[]{:S(2)}, u32[]{:S(2)}) %all-to-all-start) | async-done | bytes 294944 | tf_op jit(solution)/shard_map/while/body/eval_jaxpr/all_to_all | solution.py:121
  301.1 14.1 %conditional.3 = (bf16[72,2048]{1,0:T(8,128)(2,1)S(1)}, bf16[72]{0:T(256)(128)(2,1)S(1)}) conditional(s32[]{:T(128)} %convert_element_type.180, () %tuple.64, (bf16[8,9,2048]{2,1,0:T(8,128)(2,1)S(1)}, bf16[1024,2048]{1,0:T(8,128)(2,1)}, bf16[8,9,2048]{2,1,0:T(8,128)(2,1)S(1)}, bf16[2048,1024]{1,0:T(8,128)(2,1)}, bf16[2048,1024]{1,0:T(8,128)(2,1)}) %tuple.65), branch_computations={%region_6.6_spmd, %region_7.8_spmd} | conditional | flops 1814298624 | bytes 82280696 | solution.py:132
  329.9 13.0 %all-to-all-done.2 = bf16[8,9,2048]{2,1,0:T(8,128)(2,1)S(1)} async-done(((bf16[8,9,2048]{2,1,0:T(8,128)(2,1)}), bf16[8,9,2048]{2,1,0:T(8,128)(2,1)S(1)}, u32[]{:S(2)}, u32[]{:S(2)}) %all-to-all-start.2) | async-done | bytes 294944 | tf_op jit(solution)/shard_map/while/body/eval_jaxpr/all_to_all | solution.py:134
  357.2 13.7 %all-to-all-done.1 = bf16[8,9,2048]{2,1,0:T(8,128)(2,1)S(1)} async-done(((bf16[8,9,2048]{2,1,0:T(8,128)(2,1)}), bf16[8,9,2048]{2,1,0:T(8,128)(2,1)S(1)}, u32[]{:S(2)}, u32[]{:S(2)}) %all-to-all-start.1) | async-done | bytes 294944 | tf_op jit(solution)/shard_map/while/body/eval_jaxpr/all_to_all | solution.py:120
  374.7 14.5 %all-to-all-done = bf16[8,9,2048]{2,1,0:T(8,128)(2,1)S(1)} async-done(((bf16[8,9,2048]{2,1,0:T(8,128)(2,1)}), bf16[8,9,2048]{2,1,0:T(8,128)(2,1)S(1)}, u32[]{:S(2)}, u32[]{:S(2)}) %all-to-all-start) | async-done | bytes 294944 | tf_op jit(solution)/shard_map/while/body/eval_jaxpr/all_to_all | solution.py:121
  389.2 14.1 %conditional.3 = (bf16[72,2048]{1,0:T(8,128)(2,1)S(1)}, bf16[72]{0:T(256)(128)(2,1)S(1)}) conditional(s32[]{:T(128)} %convert_element_type.180, () %tuple.64, (bf16[8,9,2048]{2,1,0:T(8,128)(2,1)S(1)}, bf16[1024,2048]{1,0:T(8,128)(2,1)}, bf16[8,9,2048]{2,1,0:T(8,128)(2,1)S(1)}, bf16[2048,1024]{1,0:T(8,128)(2,1)}, bf16[2048,1024]{1,0:T(8,128)(2,1)}) %tuple.65), branch_computations={%region_6.6_spmd, %region_7.8_spmd} | conditional | flops 1814298624 | bytes 82280696 | solution.py:132
  445.4 13.7 %all-to-all-done.1 = bf16[8,9,2048]{2,1,0:T(8,128)(2,1)S(1)} async-done(((bf16[8,9,2048]{2,1,0:T(8,128)(2,1)}), bf16[8,9,2048]{2,1,0:T(8,128)(2,1)S(1)}, u32[]{:S(2)}, u32[]{:S(2)}) %all-to-all-start.1) | async-done | bytes 294944 | tf_op jit(solution)/shard_map/while/body/eval_jaxpr/all_to_all | solution.py:120
  462.9 14.5 %all-to-all-done = bf16[8,9,2048]{2,1,0:T(8,128)(2,1)S(1)} async-done(((bf16[8,9,2048]{2,1,0:T(8,128)(2,1)}), bf16[8,9,2048]{2,1,0:T(8,128)(2,1)S(1)}, u32[]{:S(2)}, u32[]{:S(2)}) %all-to-all-start) | async-done | bytes 294944 | tf_op jit(solution)/shard_map/while/body/eval_jaxpr/all_to_all | solution.py:121
  477.4 14.1 %conditional.3 = (bf16[72,2048]{1,0:T(8,128)(2,1)S(1)}, bf16[72]{0:T(256)(128)(2,1)S(1)}) conditional(s32[]{:T(128)} %convert_element_type.180, () %tuple.64, (bf16[8,9,2048]{2,1,0:T(8,128)(2,1)S(1)}, bf16[1024,2048]{1,0:T(8,128)(2,1)}, bf16[8,9,2048]{2,1,0:T(8,128)(2,1)S(1)}, bf16[2048,1024]{1,0:T(8,128)(2,1)}, bf16[2048,1024]{1,0:T(8,128)(2,1)}) %tuple.65), branch_computations={%region_6.6_spmd, %region_7.8_spmd} | conditional | flops 1814298624 | bytes 82280696 | solution.py:132
  533.5 13.7 %all-to-all-done.1 = bf16[8,9,2048]{2,1,0:T(8,128)(2,1)S(1)} async-done(((bf16[8,9,2048]{2,1,0:T(8,128)(2,1)}), bf16[8,9,2048]{2,1,0:T(8,128)(2,1)S(1)}, u32[]{:S(2)}, u32[]{:S(2)}) %all-to-all-start.1) | async-done | bytes 294944 | tf_op jit(solution)/shard_map/while/body/eval_jaxpr/all_to_all | solution.py:120
  551.0 14.5 %all-to-all-done = bf16[8,9,2048]{2,1,0:T(8,128)(2,1)S(1)} async-done(((bf16[8,9,2048]{2,1,0:T(8,128)(2,1)}), bf16[8,9,2048]{2,1,0:T(8,128)(2,1)S(1)}, u32[]{:S(2)}, u32[]{:S(2)}) %all-to-all-start) | async-done | bytes 294944 | tf_op jit(solution)/shard_map/while/body/eval_jaxpr/all_to_all | solution.py:121
  565.5 14.1 %conditional.3 = (bf16[72,2048]{1,0:T(8,128)(2,1)S(1)}, bf16[72]{0:T(256)(128)(2,1)S(1)}) conditional(s32[]{:T(128)} %convert_element_type.180, () %tuple.64, (bf16[8,9,2048]{2,1,0:T(8,128)(2,1)S(1)}, bf16[1024,2048]{1,0:T(8,128)(2,1)}, bf16[8,9,2048]{2,1,0:T(8,128)(2,1)S(1)}, bf16[2048,1024]{1,0:T(8,128)(2,1)}, bf16[2048,1024]{1,0:T(8,128)(2,1)}) %tuple.65), branch_computations={%region_6.6_spmd, %region_7.8_spmd} | conditional | flops 1814298624 | bytes 82280696 | solution.py:132
  621.7 13.7 %all-to-all-done.1 = bf16[8,9,2048]{2,1,0:T(8,128)(2,1)S(1)} async-done(((bf16[8,9,2048]{2,1,0:T(8,128)(2,1)}), bf16[8,9,2048]{2,1,0:T(8,128)(2,1)S(1)}, u32[]{:S(2)}, u32[]{:S(2)}) %all-to-all-start.1) | async-done | bytes 294944 | tf_op jit(solution)/shard_map/while/body/eval_jaxpr/all_to_all | solution.py:120
  639.2 14.5 %all-to-all-done = bf16[8,9,2048]{2,1,0:T(8,128)(2,1)S(1)} async-done(((bf16[8,9,2048]{2,1,0:T(8,128)(2,1)}), bf16[8,9,2048]{2,1,0:T(8,128)(2,1)S(1)}, u32[]{:S(2)}, u32[]{:S(2)}) %all-to-all-start) | async-done | bytes 294944 | tf_op jit(solution)/shard_map/while/body/eval_jaxpr/all_to_all | solution.py:121
  653.7 14.1 %conditional.3 = (bf16[72,2048]{1,0:T(8,128)(2,1)S(1)}, bf16[72]{0:T(256)(128)(2,1)S(1)}) conditional(s32[]{:T(128)} %convert_element_type.180, () %tuple.64, (bf16[8,9,2048]{2,1,0:T(8,128)(2,1)S(1)}, bf16[1024,2048]{1,0:T(8,128)(2,1)}, bf16[8,9,2048]{2,1,0:T(8,128)(2,1)S(1)}, bf16[2048,1024]{1,0:T(8,128)(2,1)}, bf16[2048,1024]{1,0:T(8,128)(2,1)}) %tuple.65), branch_computations={%region_6.6_spmd, %region_7.8_spmd} | conditional | flops 1814298624 | bytes 82280696 | solution.py:132
  709.8 13.7 %all-to-all-done.1 = bf16[8,9,2048]{2,1,0:T(8,128)(2,1)S(1)} async-done(((bf16[8,9,2048]{2,1,0:T(8,128)(2,1)}), bf16[8,9,2048]{2,1,0:T(8,128)(2,1)S(1)}, u32[]{:S(2)}, u32[]{:S(2)}) %all-to-all-start.1) | async-done | bytes 294944 | tf_op jit(solution)/shard_map/while/body/eval_jaxpr/all_to_all | solution.py:120
  727.4 14.5 %all-to-all-done = bf16[8,9,2048]{2,1,0:T(8,128)(2,1)S(1)} async-done(((bf16[8,9,2048]{2,1,0:T(8,128)(2,1)}), bf16[8,9,2048]{2,1,0:T(8,128)(2,1)S(1)}, u32[]{:S(2)}, u32[]{:S(2)}) %all-to-all-start) | async-done | bytes 294944 | tf_op jit(solution)/shard_map/while/body/eval_jaxpr/all_to_all | solution.py:121
  741.9 14.1 %conditional.3 = (bf16[72,2048]{1,0:T(8,128)(2,1)S(1)}, bf16[72]{0:T(256)(128)(2,1)S(1)}) conditional(s32[]{:T(128)} %convert_element_type.180, () %tuple.64, (bf16[8,9,2048]{2,1,0:T(8,128)(2,1)S(1)}, bf16[1024,2048]{1,0:T(8,128)(2,1)}, bf16[8,9,2048]{2,1,0:T(8,128)(2,1)S(1)}, bf16[2048,1024]{1,0:T(8,128)(2,1)}, bf16[2048,1024]{1,0:T(8,128)(2,1)}) %tuple.65), branch_computations={%region_6.6_spmd, %region_7.8_spmd} | conditional | flops 1814298624 | bytes 82280696 | solution.py:132
  794.8 13.7 %all-to-all-done.1 = bf16[8,9,2048]{2,1,0:T(8,128)(2,1)S(1)} async-done(((bf16[8,9,2048]{2,1,0:T(8,128)(2,1)}), bf16[8,9,2048]{2,1,0:T(8,128)(2,1)S(1)}, u32[]{:S(2)}, u32[]{:S(2)}) %all-to-all-start.1) | async-done | bytes 294944 | tf_op jit(solution)/shard_map/while/body/eval_jaxpr/all_to_all | solution.py:120
  812.3 14.5 %all-to-all-done = bf16[8,9,2048]{2,1,0:T(8,128)(2,1)S(1)} async-done(((bf16[8,9,2048]{2,1,0:T(8,128)(2,1)}), bf16[8,9,2048]{2,1,0:T(8,128)(2,1)S(1)}, u32[]{:S(2)}, u32[]{:S(2)}) %all-to-all-start) | async-done | bytes 294944 | tf_op jit(solution)/shard_map/while/body/eval_jaxpr/all_to_all | solution.py:121
  841.6 13.0 %all-to-all-done.2 = bf16[8,9,2048]{2,1,0:T(8,128)(2,1)S(1)} async-done(((bf16[8,9,2048]{2,1,0:T(8,128)(2,1)}), bf16[8,9,2048]{2,1,0:T(8,128)(2,1)S(1)}, u32[]{:S(2)}, u32[]{:S(2)}) %all-to-all-start.2) | async-done | bytes 294944 | tf_op jit(solution)/shard_map/while/body/eval_jaxpr/all_to_all | solution.py:134
  868.9 13.7 %all-to-all-done.1 = bf16[8,9,2048]{2,1,0:T(8,128)(2,1)S(1)} async-done(((bf16[8,9,2048]{2,1,0:T(8,128)(2,1)}), bf16[8,9,2048]{2,1,0:T(8,128)(2,1)S(1)}, u32[]{:S(2)}, u32[]{:S(2)}) %all-to-all-start.1) | async-done | bytes 294944 | tf_op jit(solution)/shard_map/while/body/eval_jaxpr/all_to_all | solution.py:120
  886.4 14.5 %all-to-all-done = bf16[8,9,2048]{2,1,0:T(8,128)(2,1)S(1)} async-done(((bf16[8,9,2048]{2,1,0:T(8,128)(2,1)}), bf16[8,9,2048]{2,1,0:T(8,128)(2,1)S(1)}, u32[]{:S(2)}, u32[]{:S(2)}) %all-to-all-start) | async-done | bytes 294944 | tf_op jit(solution)/shard_map/while/body/eval_jaxpr/all_to_all | solution.py:121
  915.6 13.0 %all-to-all-done.2 = bf16[8,9,2048]{2,1,0:T(8,128)(2,1)S(1)} async-done(((bf16[8,9,2048]{2,1,0:T(8,128)(2,1)}), bf16[8,9,2048]{2,1,0:T(8,128)(2,1)S(1)}, u32[]{:S(2)}, u32[]{:S(2)}) %all-to-all-start.2) | async-done | bytes 294944 | tf_op jit(solution)/shard_map/while/body/eval_jaxpr/all_to_all | solution.py:134
  (655 shorter events, 607.4 us)
Async XLA Ops:
  16.6 20.1 %all-to-all-start.1 = ((bf16[8,9,2048]{2,1,0:T(8,128)(2,1)}), bf16[8,9,2048]{2,1,0:T(8,128)(2,1)S(1)}, u32[]{:S(2)}, u32[]{:S(2)}) async-start(bf16[8,9,2048]{2,1,0:T(8,128)(2,1)} %reshape.265), calls=%async_computation.1 | async-start | bytes 1048576 | tf_op jit(solution)/shard_map/while/body/eval_jaxpr/all_to_all | solution.py:120
  36.7 18.2 %all-to-all-start = ((bf16[8,9,2048]{2,1,0:T(8,128)(2,1)}), bf16[8,9,2048]{2,1,0:T(8,128)(2,1)S(1)}, u32[]{:S(2)}, u32[]{:S(2)}) async-start(bf16[8,9,2048]{2,1,0:T(8,128)(2,1)} %reshape.263), calls=%async_computation | async-start | bytes 1048576 | tf_op jit(solution)/shard_map/while/body/eval_jaxpr/all_to_all | solution.py:121
  82.1 13.8 %collective-permute-start = (bf16[16,2048]{1,0:T(8,128)(2,1)S(1)}, bf16[16,2048]{1,0:T(8,128)(2,1)S(1)}, u32[]{:S(2)}, u32[]{:S(2)}) collective-permute-start(bf16[16,2048]{1,0:T(8,128)(2,1)S(1)} %broadcast_select_fusion.2), channel_id=1, source_target_pairs={{8,0},{16,8},{24,16},{9,1},{17,9},{25,17},{10,2},{18,10},{26,18},{... | collective-permute-start | bytes 196616 | tf_op jit(solution)/shard_map/while/body/eval_jaxpr/ppermute | solution.py:10
  91.1 14.7 %all-to-all-start.1 = ((bf16[8,9,2048]{2,1,0:T(8,128)(2,1)}), bf16[8,9,2048]{2,1,0:T(8,128)(2,1)S(1)}, u32[]{:S(2)}, u32[]{:S(2)}) async-start(bf16[8,9,2048]{2,1,0:T(8,128)(2,1)} %reshape.265), calls=%async_computation.1 | async-start | bytes 1048576 | tf_op jit(solution)/shard_map/while/body/eval_jaxpr/all_to_all | solution.py:120
  105.8 14.3 %all-to-all-start = ((bf16[8,9,2048]{2,1,0:T(8,128)(2,1)}), bf16[8,9,2048]{2,1,0:T(8,128)(2,1)S(1)}, u32[]{:S(2)}, u32[]{:S(2)}) async-start(bf16[8,9,2048]{2,1,0:T(8,128)(2,1)} %reshape.263), calls=%async_computation | async-start | bytes 1048576 | tf_op jit(solution)/shard_map/while/body/eval_jaxpr/all_to_all | solution.py:121
  147.4 18.9 %all-to-all-start.2 = ((bf16[8,9,2048]{2,1,0:T(8,128)(2,1)}), bf16[8,9,2048]{2,1,0:T(8,128)(2,1)S(1)}, u32[]{:S(2)}, u32[]{:S(2)}) async-start(bf16[8,9,2048]{2,1,0:T(8,128)(2,1)} %reshape.266), calls=%async_computation.2 | async-start | bytes 1048576 | tf_op jit(solution)/shard_map/while/body/eval_jaxpr/all_to_all | solution.py:134
  175.3 19.2 %all-to-all-start.1 = ((bf16[8,9,2048]{2,1,0:T(8,128)(2,1)}), bf16[8,9,2048]{2,1,0:T(8,128)(2,1)S(1)}, u32[]{:S(2)}, u32[]{:S(2)}) async-start(bf16[8,9,2048]{2,1,0:T(8,128)(2,1)} %reshape.265), calls=%async_computation.1 | async-start | bytes 1048576 | tf_op jit(solution)/shard_map/while/body/eval_jaxpr/all_to_all | solution.py:120
  194.6 18.3 %all-to-all-start = ((bf16[8,9,2048]{2,1,0:T(8,128)(2,1)}), bf16[8,9,2048]{2,1,0:T(8,128)(2,1)S(1)}, u32[]{:S(2)}, u32[]{:S(2)}) async-start(bf16[8,9,2048]{2,1,0:T(8,128)(2,1)} %reshape.263), calls=%async_computation | async-start | bytes 1048576 | tf_op jit(solution)/shard_map/while/body/eval_jaxpr/all_to_all | solution.py:121
  237.9 16.9 %all-to-all-start.2 = ((bf16[8,9,2048]{2,1,0:T(8,128)(2,1)}), bf16[8,9,2048]{2,1,0:T(8,128)(2,1)S(1)}, u32[]{:S(2)}, u32[]{:S(2)}) async-start(bf16[8,9,2048]{2,1,0:T(8,128)(2,1)} %reshape.266), calls=%async_computation.2 | async-start | bytes 1048576 | tf_op jit(solution)/shard_map/while/body/eval_jaxpr/all_to_all | solution.py:134
  263.9 18.8 %all-to-all-start.1 = ((bf16[8,9,2048]{2,1,0:T(8,128)(2,1)}), bf16[8,9,2048]{2,1,0:T(8,128)(2,1)S(1)}, u32[]{:S(2)}, u32[]{:S(2)}) async-start(bf16[8,9,2048]{2,1,0:T(8,128)(2,1)} %reshape.265), calls=%async_computation.1 | async-start | bytes 1048576 | tf_op jit(solution)/shard_map/while/body/eval_jaxpr/all_to_all | solution.py:120
  282.8 18.3 %all-to-all-start = ((bf16[8,9,2048]{2,1,0:T(8,128)(2,1)}), bf16[8,9,2048]{2,1,0:T(8,128)(2,1)S(1)}, u32[]{:S(2)}, u32[]{:S(2)}) async-start(bf16[8,9,2048]{2,1,0:T(8,128)(2,1)} %reshape.263), calls=%async_computation | async-start | bytes 1048576 | tf_op jit(solution)/shard_map/while/body/eval_jaxpr/all_to_all | solution.py:121
  326.0 16.9 %all-to-all-start.2 = ((bf16[8,9,2048]{2,1,0:T(8,128)(2,1)}), bf16[8,9,2048]{2,1,0:T(8,128)(2,1)S(1)}, u32[]{:S(2)}, u32[]{:S(2)}) async-start(bf16[8,9,2048]{2,1,0:T(8,128)(2,1)} %reshape.266), calls=%async_computation.2 | async-start | bytes 1048576 | tf_op jit(solution)/shard_map/while/body/eval_jaxpr/all_to_all | solution.py:134
  352.1 18.8 %all-to-all-start.1 = ((bf16[8,9,2048]{2,1,0:T(8,128)(2,1)}), bf16[8,9,2048]{2,1,0:T(8,128)(2,1)S(1)}, u32[]{:S(2)}, u32[]{:S(2)}) async-start(bf16[8,9,2048]{2,1,0:T(8,128)(2,1)} %reshape.265), calls=%async_computation.1 | async-start | bytes 1048576 | tf_op jit(solution)/shard_map/while/body/eval_jaxpr/all_to_all | solution.py:120
  370.9 18.3 %all-to-all-start = ((bf16[8,9,2048]{2,1,0:T(8,128)(2,1)}), bf16[8,9,2048]{2,1,0:T(8,128)(2,1)S(1)}, u32[]{:S(2)}, u32[]{:S(2)}) async-start(bf16[8,9,2048]{2,1,0:T(8,128)(2,1)} %reshape.263), calls=%async_computation | async-start | bytes 1048576 | tf_op jit(solution)/shard_map/while/body/eval_jaxpr/all_to_all | solution.py:121
  414.2 16.9 %all-to-all-start.2 = ((bf16[8,9,2048]{2,1,0:T(8,128)(2,1)}), bf16[8,9,2048]{2,1,0:T(8,128)(2,1)S(1)}, u32[]{:S(2)}, u32[]{:S(2)}) async-start(bf16[8,9,2048]{2,1,0:T(8,128)(2,1)} %reshape.266), calls=%async_computation.2 | async-start | bytes 1048576 | tf_op jit(solution)/shard_map/while/body/eval_jaxpr/all_to_all | solution.py:134
  440.2 18.8 %all-to-all-start.1 = ((bf16[8,9,2048]{2,1,0:T(8,128)(2,1)}), bf16[8,9,2048]{2,1,0:T(8,128)(2,1)S(1)}, u32[]{:S(2)}, u32[]{:S(2)}) async-start(bf16[8,9,2048]{2,1,0:T(8,128)(2,1)} %reshape.265), calls=%async_computation.1 | async-start | bytes 1048576 | tf_op jit(solution)/shard_map/while/body/eval_jaxpr/all_to_all | solution.py:120
  459.1 18.3 %all-to-all-start = ((bf16[8,9,2048]{2,1,0:T(8,128)(2,1)}), bf16[8,9,2048]{2,1,0:T(8,128)(2,1)S(1)}, u32[]{:S(2)}, u32[]{:S(2)}) async-start(bf16[8,9,2048]{2,1,0:T(8,128)(2,1)} %reshape.263), calls=%async_computation | async-start | bytes 1048576 | tf_op jit(solution)/shard_map/while/body/eval_jaxpr/all_to_all | solution.py:121
  502.3 16.9 %all-to-all-start.2 = ((bf16[8,9,2048]{2,1,0:T(8,128)(2,1)}), bf16[8,9,2048]{2,1,0:T(8,128)(2,1)S(1)}, u32[]{:S(2)}, u32[]{:S(2)}) async-start(bf16[8,9,2048]{2,1,0:T(8,128)(2,1)} %reshape.266), calls=%async_computation.2 | async-start | bytes 1048576 | tf_op jit(solution)/shard_map/while/body/eval_jaxpr/all_to_all | solution.py:134
  528.4 18.8 %all-to-all-start.1 = ((bf16[8,9,2048]{2,1,0:T(8,128)(2,1)}), bf16[8,9,2048]{2,1,0:T(8,128)(2,1)S(1)}, u32[]{:S(2)}, u32[]{:S(2)}) async-start(bf16[8,9,2048]{2,1,0:T(8,128)(2,1)} %reshape.265), calls=%async_computation.1 | async-start | bytes 1048576 | tf_op jit(solution)/shard_map/while/body/eval_jaxpr/all_to_all | solution.py:120
  547.2 18.3 %all-to-all-start = ((bf16[8,9,2048]{2,1,0:T(8,128)(2,1)}), bf16[8,9,2048]{2,1,0:T(8,128)(2,1)S(1)}, u32[]{:S(2)}, u32[]{:S(2)}) async-start(bf16[8,9,2048]{2,1,0:T(8,128)(2,1)} %reshape.263), calls=%async_computation | async-start | bytes 1048576 | tf_op jit(solution)/shard_map/while/body/eval_jaxpr/all_to_all | solution.py:121
  590.5 16.9 %all-to-all-start.2 = ((bf16[8,9,2048]{2,1,0:T(8,128)(2,1)}), bf16[8,9,2048]{2,1,0:T(8,128)(2,1)S(1)}, u32[]{:S(2)}, u32[]{:S(2)}) async-start(bf16[8,9,2048]{2,1,0:T(8,128)(2,1)} %reshape.266), calls=%async_computation.2 | async-start | bytes 1048576 | tf_op jit(solution)/shard_map/while/body/eval_jaxpr/all_to_all | solution.py:134
  616.5 18.8 %all-to-all-start.1 = ((bf16[8,9,2048]{2,1,0:T(8,128)(2,1)}), bf16[8,9,2048]{2,1,0:T(8,128)(2,1)S(1)}, u32[]{:S(2)}, u32[]{:S(2)}) async-start(bf16[8,9,2048]{2,1,0:T(8,128)(2,1)} %reshape.265), calls=%async_computation.1 | async-start | bytes 1048576 | tf_op jit(solution)/shard_map/while/body/eval_jaxpr/all_to_all | solution.py:120
  635.4 18.3 %all-to-all-start = ((bf16[8,9,2048]{2,1,0:T(8,128)(2,1)}), bf16[8,9,2048]{2,1,0:T(8,128)(2,1)S(1)}, u32[]{:S(2)}, u32[]{:S(2)}) async-start(bf16[8,9,2048]{2,1,0:T(8,128)(2,1)} %reshape.263), calls=%async_computation | async-start | bytes 1048576 | tf_op jit(solution)/shard_map/while/body/eval_jaxpr/all_to_all | solution.py:121
  678.7 16.9 %all-to-all-start.2 = ((bf16[8,9,2048]{2,1,0:T(8,128)(2,1)}), bf16[8,9,2048]{2,1,0:T(8,128)(2,1)S(1)}, u32[]{:S(2)}, u32[]{:S(2)}) async-start(bf16[8,9,2048]{2,1,0:T(8,128)(2,1)} %reshape.266), calls=%async_computation.2 | async-start | bytes 1048576 | tf_op jit(solution)/shard_map/while/body/eval_jaxpr/all_to_all | solution.py:134
  704.7 18.8 %all-to-all-start.1 = ((bf16[8,9,2048]{2,1,0:T(8,128)(2,1)}), bf16[8,9,2048]{2,1,0:T(8,128)(2,1)S(1)}, u32[]{:S(2)}, u32[]{:S(2)}) async-start(bf16[8,9,2048]{2,1,0:T(8,128)(2,1)} %reshape.265), calls=%async_computation.1 | async-start | bytes 1048576 | tf_op jit(solution)/shard_map/while/body/eval_jaxpr/all_to_all | solution.py:120
  723.6 18.3 %all-to-all-start = ((bf16[8,9,2048]{2,1,0:T(8,128)(2,1)}), bf16[8,9,2048]{2,1,0:T(8,128)(2,1)S(1)}, u32[]{:S(2)}, u32[]{:S(2)}) async-start(bf16[8,9,2048]{2,1,0:T(8,128)(2,1)} %reshape.263), calls=%async_computation | async-start | bytes 1048576 | tf_op jit(solution)/shard_map/while/body/eval_jaxpr/all_to_all | solution.py:121
  789.6 18.8 %all-to-all-start.1 = ((bf16[8,9,2048]{2,1,0:T(8,128)(2,1)}), bf16[8,9,2048]{2,1,0:T(8,128)(2,1)S(1)}, u32[]{:S(2)}, u32[]{:S(2)}) async-start(bf16[8,9,2048]{2,1,0:T(8,128)(2,1)} %reshape.265), calls=%async_computation.1 | async-start | bytes 1048576 | tf_op jit(solution)/shard_map/while/body/eval_jaxpr/all_to_all | solution.py:120
  808.5 18.3 %all-to-all-start = ((bf16[8,9,2048]{2,1,0:T(8,128)(2,1)}), bf16[8,9,2048]{2,1,0:T(8,128)(2,1)S(1)}, u32[]{:S(2)}, u32[]{:S(2)}) async-start(bf16[8,9,2048]{2,1,0:T(8,128)(2,1)} %reshape.263), calls=%async_computation | async-start | bytes 1048576 | tf_op jit(solution)/shard_map/while/body/eval_jaxpr/all_to_all | solution.py:121
  837.7 16.9 %all-to-all-start.2 = ((bf16[8,9,2048]{2,1,0:T(8,128)(2,1)}), bf16[8,9,2048]{2,1,0:T(8,128)(2,1)S(1)}, u32[]{:S(2)}, u32[]{:S(2)}) async-start(bf16[8,9,2048]{2,1,0:T(8,128)(2,1)} %reshape.266), calls=%async_computation.2 | async-start | bytes 1048576 | tf_op jit(solution)/shard_map/while/body/eval_jaxpr/all_to_all | solution.py:134
  863.7 18.8 %all-to-all-start.1 = ((bf16[8,9,2048]{2,1,0:T(8,128)(2,1)}), bf16[8,9,2048]{2,1,0:T(8,128)(2,1)S(1)}, u32[]{:S(2)}, u32[]{:S(2)}) async-start(bf16[8,9,2048]{2,1,0:T(8,128)(2,1)} %reshape.265), calls=%async_computation.1 | async-start | bytes 1048576 | tf_op jit(solution)/shard_map/while/body/eval_jaxpr/all_to_all | solution.py:120
  882.6 18.3 %all-to-all-start = ((bf16[8,9,2048]{2,1,0:T(8,128)(2,1)}), bf16[8,9,2048]{2,1,0:T(8,128)(2,1)S(1)}, u32[]{:S(2)}, u32[]{:S(2)}) async-start(bf16[8,9,2048]{2,1,0:T(8,128)(2,1)} %reshape.263), calls=%async_computation | async-start | bytes 1048576 | tf_op jit(solution)/shard_map/while/body/eval_jaxpr/all_to_all | solution.py:121
  911.7 16.9 %all-to-all-start.2 = ((bf16[8,9,2048]{2,1,0:T(8,128)(2,1)}), bf16[8,9,2048]{2,1,0:T(8,128)(2,1)S(1)}, u32[]{:S(2)}, u32[]{:S(2)}) async-start(bf16[8,9,2048]{2,1,0:T(8,128)(2,1)} %reshape.266), calls=%async_computation.2 | async-start | bytes 1048576 | tf_op jit(solution)/shard_map/while/body/eval_jaxpr/all_to_all | solution.py:134
  (59 other events, 670.3 us)
where the time goes:
time: 939 us; the launch traced here: 932 us
  waiting for transfers between devices  498 us (53%)
  starting transfers between devices  189 us (20%)
  matrix products  138 us (15%)
  local copies, waits for them, and re-layouts  60.3 us (6%)
  other arithmetic  37.8 us (4%)
    all_to_all x11, waiting for transfers between devices, advance(): lax.all_to_all(sent_grad, 'expert', split_axis=0, concat_axis=0, tiled=True)  155 us
    all_to_all x11, waiting for transfers between devices, advance(): lax.all_to_all(sent_normed, 'expert', split_axis=0, concat_axis=0, tiled=...  144 us
    all_to_all x11, waiting for transfers between devices, advance(): lax.all_to_all(returned.reshape(experts, capacity, width), 'expert', spli...  139 us
    all_to_all x11, waiting for transfers between devices, advance(): lax.all_to_all(dprob.reshape(experts, capacity).astype(jnp.bfloat16), 'ex...  58.5 us
    all_to_all x11, starting transfers between devices, advance(): lax.all_to_all(sent_normed, 'expert', split_axis=0, concat_axis=0, tiled=...  43.6 us
    all_to_all x11, starting transfers between devices, advance(): lax.all_to_all(dprob.reshape(experts, capacity).astype(jnp.bfloat16), 'ex...  42.3 us
    all_to_all x11, starting transfers between devices, advance(): lax.all_to_all(sent_grad, 'expert', split_axis=0, concat_axis=0, tiled=True)  39.9 us
    all_to_all x11, starting transfers between devices, advance(): lax.all_to_all(returned.reshape(experts, capacity, width), 'expert', spli...  38.4 us
  transfers between devices with their start and end apart: 55, of which 45 were waited for; matrix products, arithmetic and copies ran while one was open for 9% of the time, Pallas kernels for 0%

commit v1 on v0

--- a/solution.py
+++ b/solution.py
@@ -2,6 +2,29 @@
 import jax.numpy as jnp
 from jax import lax
 from jax.sharding import PartitionSpec as P
+
+
+def cut_along(x, dim, devices):
+    lengths = x.shape
+    blocks = x.reshape(*lengths[:dim], devices, lengths[dim] // devices, *lengths[dim + 1 :])
+    return jnp.moveaxis(blocks, dim, 0)
+
+
+def joined_along(pieces, dim):
+    lengths = list(pieces.shape[1:])
+    lengths[dim] *= pieces.shape[0]
+    return jnp.moveaxis(pieces, 0, dim).reshape(lengths)
+
+
+def pairwise_exchange(x, axis, split_dim, concat_dim):
+    devices, index = (lax.axis_size(axis), lax.axis_index(axis))
+    pieces = cut_along(x, split_dim, devices)
+    done = [pieces[index]]
+    for turn in range(1, devices):
+        sent = pieces[index ^ turn]
+        done.append(lax.ppermute(sent, axis, [(i, i ^ turn) for i in range(devices)]))
+    pieces = jnp.stack(done)[index ^ jnp.arange(devices)]
+    return joined_along(pieces, concat_dim)
 
 
 def shifted(shard, axis, by):
@@ -118,7 +141,7 @@
         sent_grad = pack_rows(select, grad_in, per_token).reshape(experts, capacity, width)
         got_normed, got_grad = (
             lax.all_to_all(sent_normed, "expert", split_axis=0, concat_axis=0, tiled=True),
-            lax.all_to_all(sent_grad, "expert", split_axis=0, concat_axis=0, tiled=True),
+            pairwise_exchange(sent_grad, "expert", 0, 0),
         )
         rows_normed = got_normed.reshape(slots, width)
         rows_grad = got_grad.reshape(slots, width)

time: 939 us -> 834 us (0.89)
  waiting for transfers between devices: 498 us -> 298 us
  starting transfers between devices: 189 us -> 304 us
  local copies, waits for them, and re-layouts: 60.3 us -> 49.1 us
  matrix products: 138 us -> 127 us
    all_to_all x11 -> x0, waiting for transfers between devices: 155 us -> none  [advance(): lax.all_to_all(sent_grad, 'expert', split_axis=0, concat_axis=0, tiled=True)]
    ppermute x0 -> x77, starting transfers between devices: none -> 152 us  [pairwise_exchange(): lax.ppermute(sent, axis, [(i, i ^ turn) for i in range(devices)])]
    all_to_all x11, waiting for transfers between devices: 144 us -> 0.03 us  [advance(): lax.all_to_all(sent_normed, 'expert', split_axis=0, concat_axis=0, tiled=...]
    ppermute x0 -> x77, waiting for transfers between devices: none -> 100 us  [pairwise_exchange(): lax.ppermute(sent, axis, [(i, i ^ turn) for i in range(devices)])]
    all_to_all x11 -> x0, starting transfers between devices: 39.9 us -> none  [advance(): lax.all_to_all(sent_grad, 'expert', split_axis=0, concat_axis=0, tiled=True)]
    dot_general x8, matrix products: 28.7 us -> 11.3 us  [expert_rows(): lax.dot_general(grad_rows, down_w, (((1,), (1,)), ((), ())), preferred_el...]
  transfers between devices with their start and end apart: 55 -> 121, of which waited for: 45 -> 44; matrix products, arithmetic and copies ran while one was open for 9% -> 9% of each run, Pallas kernels for 0% -> 0%
where the time goes in v1:
time: 834 us; the launch traced here: 828 us
  starting transfers between devices  304 us (36%)
  waiting for transfers between devices  298 us (36%)
  matrix products  127 us (15%)
  local copies, waits for them, and re-layouts  49.1 us (6%)
  other arithmetic  37.9 us (5%)
    ppermute x77, starting transfers between devices, pairwise_exchange(): lax.ppermute(sent, axis, [(i, i ^ turn) for i in range(devices)])  152 us
    all_to_all x11, waiting for transfers between devices, advance(): lax.all_to_all(returned.reshape(experts, capacity, width), 'expert', spli...  139 us
    ppermute x77, waiting for transfers between devices, pairwise_exchange(): lax.ppermute(sent, axis, [(i, i ^ turn) for i in range(devices)])  100 us
    all_to_all x11, waiting for transfers between devices, advance(): lax.all_to_all(dprob.reshape(experts, capacity).astype(jnp.bfloat16), 'ex...  58.5 us
    all_to_all x11, starting transfers between devices, advance(): lax.all_to_all(dprob.reshape(experts, capacity).astype(jnp.bfloat16), 'ex...  46.1 us
    all_to_all x11, starting transfers between devices, advance(): lax.all_to_all(sent_normed, 'expert', split_axis=0, concat_axis=0, tiled=...  43.2 us
    all_to_all x11, starting transfers between devices, advance(): lax.all_to_all(returned.reshape(experts, capacity, width), 'expert', spli...  38.4 us
    dot_general x8, matrix products, expert_rows(): gate = jnp.dot(normed_rows, gate_w, preferred_element_type=jnp.float32)  25.6 us
  transfers between devices with their start and end apart: 121, of which 44 were waited for; matrix products, arithmetic and copies ran while one was open for 9% of the time, Pallas kernels for 0%

profile of v1, /device:TPU:2, one launch (start us, length us, event | category | flops | bytes accessed | tf_op | source)
XLA Modules:
  0.0 828.0 jit_solution(6105910699416392118)
XLA Ops:
  1.5 7.0 all_gather.3
  8.6 818.6 %while.18 = (s32[]{:T(128)}, bf16[16,2048]{1,0:T(8,128)(2,1)S(1)}, bf16[8,16,2048]{2,1,0:T(8,128)(2,1)S(1)}, pred[]{:T(512)}, s32[]{:T(128)}, /*index=5*/bf16[8,...) while((s32[]{:T(128)}, bf16[16,2048]{1,0:T(8,128)(2,1)S(1)}, ...), condition=%wide.region_13.14_spmd.clone, body=%wide.region_0.13_spmd.clone.sunk | while | flops 1876002688 | bytes 95948784 | solution.py:196
  37.0 7.0 collective-permute-done.4
  60.5 9.8 %all-to-all-done.1 = bf16[8,9,2048]{2,1,0:T(8,128)(2,1)S(1)} async-done(((bf16[8,9,2048]{2,1,0:T(8,128)(2,1)}), bf16[8,9,2048]{2,1,0:T(8,128)(2,1)S(1)}, u32[]{:S(2)}, u32[]{:S(2)}) %all-to-all-start.1) | async-done | bytes 294944 | tf_op jit(solution)/shard_map/while/body/eval_jaxpr/all_to_all | solution.py:157
  106.4 12.4 %conditional.3 = (bf16[72,2048]{1,0:T(8,128)(2,1)S(1)}, bf16[72]{0:T(256)(128)(2,1)S(1)}) conditional(s32[]{:T(128)} %convert_element_type.185, () %tuple.80, (s32[]{:T(128)}, s32[8,1]{0,1:T(1,128)S(1)}, bf16[8,1,9,2048]{3,2,0,1:T(8,128)(2,1)S(1)}, bf16[1024,2048]{1,0:T(8,128)(2,1)}, bf16[8,9,2048]{2,1,0:T(8,128)(2,1)S(1)}, ...), branch_computations={%region_6.6_spmd, %region_7.8_spmd} | conditional | flops 1814299648 | bytes 82874744 | solution.py:155
  119.4 7.4 all-to-all-start.2
  137.3 14.9 %all-to-all-done.1 = bf16[8,9,2048]{2,1,0:T(8,128)(2,1)S(1)} async-done(((bf16[8,9,2048]{2,1,0:T(8,128)(2,1)}), bf16[8,9,2048]{2,1,0:T(8,128)(2,1)S(1)}, u32[]{:S(2)}, u32[]{:S(2)}) %all-to-all-start.1) | async-done | bytes 294944 | tf_op jit(solution)/shard_map/while/body/eval_jaxpr/all_to_all | solution.py:157
  180.1 7.1 collective-permute-done.4
  189.5 12.4 %conditional.3 = (bf16[72,2048]{1,0:T(8,128)(2,1)S(1)}, bf16[72]{0:T(256)(128)(2,1)S(1)}) conditional(s32[]{:T(128)} %convert_element_type.185, () %tuple.80, (s32[]{:T(128)}, s32[8,1]{0,1:T(1,128)S(1)}, bf16[8,1,9,2048]{3,2,0,1:T(8,128)(2,1)S(1)}, bf16[1024,2048]{1,0:T(8,128)(2,1)}, bf16[8,9,2048]{2,1,0:T(8,128)(2,1)S(1)}, ...), branch_computations={%region_6.6_spmd, %region_7.8_spmd} | conditional | flops 1814299648 | bytes 82874744 | solution.py:155
  216.9 13.0 %all-to-all-done.1 = bf16[8,9,2048]{2,1,0:T(8,128)(2,1)S(1)} async-done(((bf16[8,9,2048]{2,1,0:T(8,128)(2,1)}), bf16[8,9,2048]{2,1,0:T(8,128)(2,1)S(1)}, u32[]{:S(2)}, u32[]{:S(2)}) %all-to-all-start.1) | async-done | bytes 294944 | tf_op jit(solution)/shard_map/while/body/eval_jaxpr/all_to_all | solution.py:157
  257.9 7.1 collective-permute-done.4
  267.4 12.4 %conditional.3 = (bf16[72,2048]{1,0:T(8,128)(2,1)S(1)}, bf16[72]{0:T(256)(128)(2,1)S(1)}) conditional(s32[]{:T(128)} %convert_element_type.185, () %tuple.80, (s32[]{:T(128)}, s32[8,1]{0,1:T(1,128)S(1)}, bf16[8,1,9,2048]{3,2,0,1:T(8,128)(2,1)S(1)}, bf16[1024,2048]{1,0:T(8,128)(2,1)}, bf16[8,9,2048]{2,1,0:T(8,128)(2,1)S(1)}, ...), branch_computations={%region_6.6_spmd, %region_7.8_spmd} | conditional | flops 1814299648 | bytes 82874744 | solution.py:155
  294.8 13.0 %all-to-all-done.1 = bf16[8,9,2048]{2,1,0:T(8,128)(2,1)S(1)} async-done(((bf16[8,9,2048]{2,1,0:T(8,128)(2,1)}), bf16[8,9,2048]{2,1,0:T(8,128)(2,1)S(1)}, u32[]{:S(2)}, u32[]{:S(2)}) %all-to-all-start.1) | async-done | bytes 294944 | tf_op jit(solution)/shard_map/while/body/eval_jaxpr/all_to_all | solution.py:157
  335.7 7.1 collective-permute-done.4
  345.2 12.4 %conditional.3 = (bf16[72,2048]{1,0:T(8,128)(2,1)S(1)}, bf16[72]{0:T(256)(128)(2,1)S(1)}) conditional(s32[]{:T(128)} %convert_element_type.185, () %tuple.80, (s32[]{:T(128)}, s32[8,1]{0,1:T(1,128)S(1)}, bf16[8,1,9,2048]{3,2,0,1:T(8,128)(2,1)S(1)}, bf16[1024,2048]{1,0:T(8,128)(2,1)}, bf16[8,9,2048]{2,1,0:T(8,128)(2,1)S(1)}, ...), branch_computations={%region_6.6_spmd, %region_7.8_spmd} | conditional | flops 1814299648 | bytes 82874744 | solution.py:155
  372.6 13.0 %all-to-all-done.1 = bf16[8,9,2048]{2,1,0:T(8,128)(2,1)S(1)} async-done(((bf16[8,9,2048]{2,1,0:T(8,128)(2,1)}), bf16[8,9,2048]{2,1,0:T(8,128)(2,1)S(1)}, u32[]{:S(2)}, u32[]{:S(2)}) %all-to-all-start.1) | async-done | bytes 294944 | tf_op jit(solution)/shard_map/while/body/eval_jaxpr/all_to_all | solution.py:157
  413.6 7.1 collective-permute-done.4
  423.0 12.4 %conditional.3 = (bf16[72,2048]{1,0:T(8,128)(2,1)S(1)}, bf16[72]{0:T(256)(128)(2,1)S(1)}) conditional(s32[]{:T(128)} %convert_element_type.185, () %tuple.80, (s32[]{:T(128)}, s32[8,1]{0,1:T(1,128)S(1)}, bf16[8,1,9,2048]{3,2,0,1:T(8,128)(2,1)S(1)}, bf16[1024,2048]{1,0:T(8,128)(2,1)}, bf16[8,9,2048]{2,1,0:T(8,128)(2,1)S(1)}, ...), branch_computations={%region_6.6_spmd, %region_7.8_spmd} | conditional | flops 1814299648 | bytes 82874744 | solution.py:155
  450.4 13.0 %all-to-all-done.1 = bf16[8,9,2048]{2,1,0:T(8,128)(2,1)S(1)} async-done(((bf16[8,9,2048]{2,1,0:T(8,128)(2,1)}), bf16[8,9,2048]{2,1,0:T(8,128)(2,1)S(1)}, u32[]{:S(2)}, u32[]{:S(2)}) %all-to-all-start.1) | async-done | bytes 294944 | tf_op jit(solution)/shard_map/while/body/eval_jaxpr/all_to_all | solution.py:157
  491.4 7.1 collective-permute-done.4
  500.8 12.4 %conditional.3 = (bf16[72,2048]{1,0:T(8,128)(2,1)S(1)}, bf16[72]{0:T(256)(128)(2,1)S(1)}) conditional(s32[]{:T(128)} %convert_element_type.185, () %tuple.80, (s32[]{:T(128)}, s32[8,1]{0,1:T(1,128)S(1)}, bf16[8,1,9,2048]{3,2,0,1:T(8,128)(2,1)S(1)}, bf16[1024,2048]{1,0:T(8,128)(2,1)}, bf16[8,9,2048]{2,1,0:T(8,128)(2,1)S(1)}, ...), branch_computations={%region_6.6_spmd, %region_7.8_spmd} | conditional | flops 1814299648 | bytes 82874744 | solution.py:155
  528.2 13.0 %all-to-all-done.1 = bf16[8,9,2048]{2,1,0:T(8,128)(2,1)S(1)} async-done(((bf16[8,9,2048]{2,1,0:T(8,128)(2,1)}), bf16[8,9,2048]{2,1,0:T(8,128)(2,1)S(1)}, u32[]{:S(2)}, u32[]{:S(2)}) %all-to-all-start.1) | async-done | bytes 294944 | tf_op jit(solution)/shard_map/while/body/eval_jaxpr/all_to_all | solution.py:157
  569.2 7.1 collective-permute-done.4
  578.6 12.4 %conditional.3 = (bf16[72,2048]{1,0:T(8,128)(2,1)S(1)}, bf16[72]{0:T(256)(128)(2,1)S(1)}) conditional(s32[]{:T(128)} %convert_element_type.185, () %tuple.80, (s32[]{:T(128)}, s32[8,1]{0,1:T(1,128)S(1)}, bf16[8,1,9,2048]{3,2,0,1:T(8,128)(2,1)S(1)}, bf16[1024,2048]{1,0:T(8,128)(2,1)}, bf16[8,9,2048]{2,1,0:T(8,128)(2,1)S(1)}, ...), branch_computations={%region_6.6_spmd, %region_7.8_spmd} | conditional | flops 1814299648 | bytes 82874744 | solution.py:155
  606.0 13.0 %all-to-all-done.1 = bf16[8,9,2048]{2,1,0:T(8,128)(2,1)S(1)} async-done(((bf16[8,9,2048]{2,1,0:T(8,128)(2,1)}), bf16[8,9,2048]{2,1,0:T(8,128)(2,1)S(1)}, u32[]{:S(2)}, u32[]{:S(2)}) %all-to-all-start.1) | async-done | bytes 294944 | tf_op jit(solution)/shard_map/while/body/eval_jaxpr/all_to_all | solution.py:157
  647.0 7.1 collective-permute-done.4
  656.5 12.4 %conditional.3 = (bf16[72,2048]{1,0:T(8,128)(2,1)S(1)}, bf16[72]{0:T(256)(128)(2,1)S(1)}) conditional(s32[]{:T(128)} %convert_element_type.185, () %tuple.80, (s32[]{:T(128)}, s32[8,1]{0,1:T(1,128)S(1)}, bf16[8,1,9,2048]{3,2,0,1:T(8,128)(2,1)S(1)}, bf16[1024,2048]{1,0:T(8,128)(2,1)}, bf16[8,9,2048]{2,1,0:T(8,128)(2,1)S(1)}, ...), branch_computations={%region_6.6_spmd, %region_7.8_spmd} | conditional | flops 1814299648 | bytes 82874744 | solution.py:155
  683.9 9.8 %all-to-all-done.1 = bf16[8,9,2048]{2,1,0:T(8,128)(2,1)S(1)} async-done(((bf16[8,9,2048]{2,1,0:T(8,128)(2,1)}), bf16[8,9,2048]{2,1,0:T(8,128)(2,1)S(1)}, u32[]{:S(2)}, u32[]{:S(2)}) %all-to-all-start.1) | async-done | bytes 294944 | tf_op jit(solution)/shard_map/while/body/eval_jaxpr/all_to_all | solution.py:157
  721.6 7.1 collective-permute-done.4
  746.1 13.0 %all-to-all-done.1 = bf16[8,9,2048]{2,1,0:T(8,128)(2,1)S(1)} async-done(((bf16[8,9,2048]{2,1,0:T(8,128)(2,1)}), bf16[8,9,2048]{2,1,0:T(8,128)(2,1)S(1)}, u32[]{:S(2)}, u32[]{:S(2)}) %all-to-all-start.1) | async-done | bytes 294944 | tf_op jit(solution)/shard_map/while/body/eval_jaxpr/all_to_all | solution.py:157
  787.1 7.1 collective-permute-done.4
  811.6 13.0 %all-to-all-done.1 = bf16[8,9,2048]{2,1,0:T(8,128)(2,1)S(1)} async-done(((bf16[8,9,2048]{2,1,0:T(8,128)(2,1)}), bf16[8,9,2048]{2,1,0:T(8,128)(2,1)S(1)}, u32[]{:S(2)}, u32[]{:S(2)}) %all-to-all-start.1) | async-done | bytes 294944 | tf_op jit(solution)/shard_map/while/body/eval_jaxpr/all_to_all | solution.py:157
  (910 shorter events, 600.2 us)
Async XLA Ops:
  15.3 30.5 %all-to-all-start = ((bf16[8,9,2048]{2,1,0:T(8,128)(2,1)}), bf16[8,9,2048]{2,1,0:T(8,128)(2,1)S(1)}, u32[]{:S(2)}, u32[]{:S(2)}) async-start(bf16[8,9,2048]{2,1,0:T(8,128)(2,1)} %reshape.281), calls=%async_computation | async-start | bytes 1048576 | tf_op jit(solution)/shard_map/while/body/eval_jaxpr/all_to_all | solution.py:143
  26.5 17.5 %collective-permute-start.4 = (bf16[1,9,2048]{2,1,0:T(8,128)(2,1)S(1)}, bf16[1,9,2048]{2,1,0:T(8,128)(2,1)S(1)}, u32[]{:S(2)}, u32[]{:S(2)}) collective-permute-start(bf16[1,9,2048]{2,1,0:T(8,128)(2,1)S(1)} %get-tuple-element.569), channel_id=1, source_target_pairs={{0,4},{1,5},{2,6},{3,7},{4,0},{5,1},{6,2},{7,3},{8,12},{9,13},{10,... | collective-permute-start | bytes 110600 | tf_op jit(solution)/shard_map/while/body/eval_jaxpr/ppermute | solution.py:25
  81.1 25.2 %all-to-all-start = ((bf16[8,9,2048]{2,1,0:T(8,128)(2,1)}), bf16[8,9,2048]{2,1,0:T(8,128)(2,1)S(1)}, u32[]{:S(2)}, u32[]{:S(2)}) async-start(bf16[8,9,2048]{2,1,0:T(8,128)(2,1)} %reshape.281), calls=%async_computation | async-start | bytes 1048576 | tf_op jit(solution)/shard_map/while/body/eval_jaxpr/all_to_all | solution.py:143
  133.3 18.8 %all-to-all-start.1 = ((bf16[8,9,2048]{2,1,0:T(8,128)(2,1)}), bf16[8,9,2048]{2,1,0:T(8,128)(2,1)S(1)}, u32[]{:S(2)}, u32[]{:S(2)}) async-start(bf16[8,9,2048]{2,1,0:T(8,128)(2,1)} %reshape.282), calls=%async_computation.1 | async-start | bytes 1048576 | tf_op jit(solution)/shard_map/while/body/eval_jaxpr/all_to_all | solution.py:157
  160.6 28.9 %all-to-all-start = ((bf16[8,9,2048]{2,1,0:T(8,128)(2,1)}), bf16[8,9,2048]{2,1,0:T(8,128)(2,1)S(1)}, u32[]{:S(2)}, u32[]{:S(2)}) async-start(bf16[8,9,2048]{2,1,0:T(8,128)(2,1)} %reshape.281), calls=%async_computation | async-start | bytes 1048576 | tf_op jit(solution)/shard_map/while/body/eval_jaxpr/all_to_all | solution.py:143
  169.6 17.5 %collective-permute-start.4 = (bf16[1,9,2048]{2,1,0:T(8,128)(2,1)S(1)}, bf16[1,9,2048]{2,1,0:T(8,128)(2,1)S(1)}, u32[]{:S(2)}, u32[]{:S(2)}) collective-permute-start(bf16[1,9,2048]{2,1,0:T(8,128)(2,1)S(1)} %get-tuple-element.569), channel_id=1, source_target_pairs={{0,4},{1,5},{2,6},{3,7},{4,0},{5,1},{6,2},{7,3},{8,12},{9,13},{10,... | collective-permute-start | bytes 110600 | tf_op jit(solution)/shard_map/while/body/eval_jaxpr/ppermute | solution.py:25
  172.4 17.0 %collective-permute-start.5 = (bf16[1,9,2048]{2,1,0:T(8,128)(2,1)S(1)}, bf16[1,9,2048]{2,1,0:T(8,128)(2,1)S(1)}, u32[]{:S(2)}, u32[]{:S(2)}) collective-permute-start(bf16[1,9,2048]{2,1,0:T(8,128)(2,1)S(1)} %get-tuple-element.570), channel_id=1, source_target_pairs={{0,5},{1,4},{2,7},{3,6},{4,1},{5,0},{6,3},{7,2},{8,13},{9,12},{10,... | collective-permute-start | bytes 110600 | tf_op jit(solution)/shard_map/while/body/eval_jaxpr/ppermute | solution.py:25
  213.0 16.9 %all-to-all-start.1 = ((bf16[8,9,2048]{2,1,0:T(8,128)(2,1)}), bf16[8,9,2048]{2,1,0:T(8,128)(2,1)S(1)}, u32[]{:S(2)}, u32[]{:S(2)}) async-start(bf16[8,9,2048]{2,1,0:T(8,128)(2,1)} %reshape.282), calls=%async_computation.1 | async-start | bytes 1048576 | tf_op jit(solution)/shard_map/while/body/eval_jaxpr/all_to_all | solution.py:157
  238.4 28.9 %all-to-all-start = ((bf16[8,9,2048]{2,1,0:T(8,128)(2,1)}), bf16[8,9,2048]{2,1,0:T(8,128)(2,1)S(1)}, u32[]{:S(2)}, u32[]{:S(2)}) async-start(bf16[8,9,2048]{2,1,0:T(8,128)(2,1)} %reshape.281), calls=%async_computation | async-start | bytes 1048576 | tf_op jit(solution)/shard_map/while/body/eval_jaxpr/all_to_all | solution.py:143
  247.4 17.5 %collective-permute-start.4 = (bf16[1,9,2048]{2,1,0:T(8,128)(2,1)S(1)}, bf16[1,9,2048]{2,1,0:T(8,128)(2,1)S(1)}, u32[]{:S(2)}, u32[]{:S(2)}) collective-permute-start(bf16[1,9,2048]{2,1,0:T(8,128)(2,1)S(1)} %get-tuple-element.569), channel_id=1, source_target_pairs={{0,4},{1,5},{2,6},{3,7},{4,0},{5,1},{6,2},{7,3},{8,12},{9,13},{10,... | collective-permute-start | bytes 110600 | tf_op jit(solution)/shard_map/while/body/eval_jaxpr/ppermute | solution.py:25
  250.3 17.0 %collective-permute-start.5 = (bf16[1,9,2048]{2,1,0:T(8,128)(2,1)S(1)}, bf16[1,9,2048]{2,1,0:T(8,128)(2,1)S(1)}, u32[]{:S(2)}, u32[]{:S(2)}) collective-permute-start(bf16[1,9,2048]{2,1,0:T(8,128)(2,1)S(1)} %get-tuple-element.570), channel_id=1, source_target_pairs={{0,5},{1,4},{2,7},{3,6},{4,1},{5,0},{6,3},{7,2},{8,13},{9,12},{10,... | collective-permute-start | bytes 110600 | tf_op jit(solution)/shard_map/while/body/eval_jaxpr/ppermute | solution.py:25
  316.2 28.9 %all-to-all-start = ((bf16[8,9,2048]{2,1,0:T(8,128)(2,1)}), bf16[8,9,2048]{2,1,0:T(8,128)(2,1)S(1)}, u32[]{:S(2)}, u32[]{:S(2)}) async-start(bf16[8,9,2048]{2,1,0:T(8,128)(2,1)} %reshape.281), calls=%async_computation | async-start | bytes 1048576 | tf_op jit(solution)/shard_map/while/body/eval_jaxpr/all_to_all | solution.py:143
  325.3 17.5 %collective-permute-start.4 = (bf16[1,9,2048]{2,1,0:T(8,128)(2,1)S(1)}, bf16[1,9,2048]{2,1,0:T(8,128)(2,1)S(1)}, u32[]{:S(2)}, u32[]{:S(2)}) collective-permute-start(bf16[1,9,2048]{2,1,0:T(8,128)(2,1)S(1)} %get-tuple-element.569), channel_id=1, source_target_pairs={{0,4},{1,5},{2,6},{3,7},{4,0},{5,1},{6,2},{7,3},{8,12},{9,13},{10,... | collective-permute-start | bytes 110600 | tf_op jit(solution)/shard_map/while/body/eval_jaxpr/ppermute | solution.py:25
  328.1 17.0 %collective-permute-start.5 = (bf16[1,9,2048]{2,1,0:T(8,128)(2,1)S(1)}, bf16[1,9,2048]{2,1,0:T(8,128)(2,1)S(1)}, u32[]{:S(2)}, u32[]{:S(2)}) collective-permute-start(bf16[1,9,2048]{2,1,0:T(8,128)(2,1)S(1)} %get-tuple-element.570), channel_id=1, source_target_pairs={{0,5},{1,4},{2,7},{3,6},{4,1},{5,0},{6,3},{7,2},{8,13},{9,12},{10,... | collective-permute-start | bytes 110600 | tf_op jit(solution)/shard_map/while/body/eval_jaxpr/ppermute | solution.py:25
  394.0 28.9 %all-to-all-start = ((bf16[8,9,2048]{2,1,0:T(8,128)(2,1)}), bf16[8,9,2048]{2,1,0:T(8,128)(2,1)S(1)}, u32[]{:S(2)}, u32[]{:S(2)}) async-start(bf16[8,9,2048]{2,1,0:T(8,128)(2,1)} %reshape.281), calls=%async_computation | async-start | bytes 1048576 | tf_op jit(solution)/shard_map/while/body/eval_jaxpr/all_to_all | solution.py:143
  403.1 17.5 %collective-permute-start.4 = (bf16[1,9,2048]{2,1,0:T(8,128)(2,1)S(1)}, bf16[1,9,2048]{2,1,0:T(8,128)(2,1)S(1)}, u32[]{:S(2)}, u32[]{:S(2)}) collective-permute-start(bf16[1,9,2048]{2,1,0:T(8,128)(2,1)S(1)} %get-tuple-element.569), channel_id=1, source_target_pairs={{0,4},{1,5},{2,6},{3,7},{4,0},{5,1},{6,2},{7,3},{8,12},{9,13},{10,... | collective-permute-start | bytes 110600 | tf_op jit(solution)/shard_map/while/body/eval_jaxpr/ppermute | solution.py:25
  405.9 17.0 %collective-permute-start.5 = (bf16[1,9,2048]{2,1,0:T(8,128)(2,1)S(1)}, bf16[1,9,2048]{2,1,0:T(8,128)(2,1)S(1)}, u32[]{:S(2)}, u32[]{:S(2)}) collective-permute-start(bf16[1,9,2048]{2,1,0:T(8,128)(2,1)S(1)} %get-tuple-element.570), channel_id=1, source_target_pairs={{0,5},{1,4},{2,7},{3,6},{4,1},{5,0},{6,3},{7,2},{8,13},{9,12},{10,... | collective-permute-start | bytes 110600 | tf_op jit(solution)/shard_map/while/body/eval_jaxpr/ppermute | solution.py:25
  471.9 28.9 %all-to-all-start = ((bf16[8,9,2048]{2,1,0:T(8,128)(2,1)}), bf16[8,9,2048]{2,1,0:T(8,128)(2,1)S(1)}, u32[]{:S(2)}, u32[]{:S(2)}) async-start(bf16[8,9,2048]{2,1,0:T(8,128)(2,1)} %reshape.281), calls=%async_computation | async-start | bytes 1048576 | tf_op jit(solution)/shard_map/while/body/eval_jaxpr/all_to_all | solution.py:143
  480.9 17.5 %collective-permute-start.4 = (bf16[1,9,2048]{2,1,0:T(8,128)(2,1)S(1)}, bf16[1,9,2048]{2,1,0:T(8,128)(2,1)S(1)}, u32[]{:S(2)}, u32[]{:S(2)}) collective-permute-start(bf16[1,9,2048]{2,1,0:T(8,128)(2,1)S(1)} %get-tuple-element.569), channel_id=1, source_target_pairs={{0,4},{1,5},{2,6},{3,7},{4,0},{5,1},{6,2},{7,3},{8,12},{9,13},{10,... | collective-permute-start | bytes 110600 | tf_op jit(solution)/shard_map/while/body/eval_jaxpr/ppermute | solution.py:25
  483.7 17.0 %collective-permute-start.5 = (bf16[1,9,2048]{2,1,0:T(8,128)(2,1)S(1)}, bf16[1,9,2048]{2,1,0:T(8,128)(2,1)S(1)}, u32[]{:S(2)}, u32[]{:S(2)}) collective-permute-start(bf16[1,9,2048]{2,1,0:T(8,128)(2,1)S(1)} %get-tuple-element.570), channel_id=1, source_target_pairs={{0,5},{1,4},{2,7},{3,6},{4,1},{5,0},{6,3},{7,2},{8,13},{9,12},{10,... | collective-permute-start | bytes 110600 | tf_op jit(solution)/shard_map/while/body/eval_jaxpr/ppermute | solution.py:25
  549.7 28.9 %all-to-all-start = ((bf16[8,9,2048]{2,1,0:T(8,128)(2,1)}), bf16[8,9,2048]{2,1,0:T(8,128)(2,1)S(1)}, u32[]{:S(2)}, u32[]{:S(2)}) async-start(bf16[8,9,2048]{2,1,0:T(8,128)(2,1)} %reshape.281), calls=%async_computation | async-start | bytes 1048576 | tf_op jit(solution)/shard_map/while/body/eval_jaxpr/all_to_all | solution.py:143
  558.7 17.5 %collective-permute-start.4 = (bf16[1,9,2048]{2,1,0:T(8,128)(2,1)S(1)}, bf16[1,9,2048]{2,1,0:T(8,128)(2,1)S(1)}, u32[]{:S(2)}, u32[]{:S(2)}) collective-permute-start(bf16[1,9,2048]{2,1,0:T(8,128)(2,1)S(1)} %get-tuple-element.569), channel_id=1, source_target_pairs={{0,4},{1,5},{2,6},{3,7},{4,0},{5,1},{6,2},{7,3},{8,12},{9,13},{10,... | collective-permute-start | bytes 110600 | tf_op jit(solution)/shard_map/while/body/eval_jaxpr/ppermute | solution.py:25
  561.6 17.0 %collective-permute-start.5 = (bf16[1,9,2048]{2,1,0:T(8,128)(2,1)S(1)}, bf16[1,9,2048]{2,1,0:T(8,128)(2,1)S(1)}, u32[]{:S(2)}, u32[]{:S(2)}) collective-permute-start(bf16[1,9,2048]{2,1,0:T(8,128)(2,1)S(1)} %get-tuple-element.570), channel_id=1, source_target_pairs={{0,5},{1,4},{2,7},{3,6},{4,1},{5,0},{6,3},{7,2},{8,13},{9,12},{10,... | collective-permute-start | bytes 110600 | tf_op jit(solution)/shard_map/while/body/eval_jaxpr/ppermute | solution.py:25
  627.5 28.9 %all-to-all-start = ((bf16[8,9,2048]{2,1,0:T(8,128)(2,1)}), bf16[8,9,2048]{2,1,0:T(8,128)(2,1)S(1)}, u32[]{:S(2)}, u32[]{:S(2)}) async-start(bf16[8,9,2048]{2,1,0:T(8,128)(2,1)} %reshape.281), calls=%async_computation | async-start | bytes 1048576 | tf_op jit(solution)/shard_map/while/body/eval_jaxpr/all_to_all | solution.py:143
  636.5 17.5 %collective-permute-start.4 = (bf16[1,9,2048]{2,1,0:T(8,128)(2,1)S(1)}, bf16[1,9,2048]{2,1,0:T(8,128)(2,1)S(1)}, u32[]{:S(2)}, u32[]{:S(2)}) collective-permute-start(bf16[1,9,2048]{2,1,0:T(8,128)(2,1)S(1)} %get-tuple-element.569), channel_id=1, source_target_pairs={{0,4},{1,5},{2,6},{3,7},{4,0},{5,1},{6,2},{7,3},{8,12},{9,13},{10,... | collective-permute-start | bytes 110600 | tf_op jit(solution)/shard_map/while/body/eval_jaxpr/ppermute | solution.py:25
  639.4 17.0 %collective-permute-start.5 = (bf16[1,9,2048]{2,1,0:T(8,128)(2,1)S(1)}, bf16[1,9,2048]{2,1,0:T(8,128)(2,1)S(1)}, u32[]{:S(2)}, u32[]{:S(2)}) collective-permute-start(bf16[1,9,2048]{2,1,0:T(8,128)(2,1)S(1)} %get-tuple-element.570), channel_id=1, source_target_pairs={{0,5},{1,4},{2,7},{3,6},{4,1},{5,0},{6,3},{7,2},{8,13},{9,12},{10,... | collective-permute-start | bytes 110600 | tf_op jit(solution)/shard_map/while/body/eval_jaxpr/ppermute | solution.py:25
  702.1 28.9 %all-to-all-start = ((bf16[8,9,2048]{2,1,0:T(8,128)(2,1)}), bf16[8,9,2048]{2,1,0:T(8,128)(2,1)S(1)}, u32[]{:S(2)}, u32[]{:S(2)}) async-start(bf16[8,9,2048]{2,1,0:T(8,128)(2,1)} %reshape.281), calls=%async_computation | async-start | bytes 1048576 | tf_op jit(solution)/shard_map/while/body/eval_jaxpr/all_to_all | solution.py:143
  711.1 17.5 %collective-permute-start.4 = (bf16[1,9,2048]{2,1,0:T(8,128)(2,1)S(1)}, bf16[1,9,2048]{2,1,0:T(8,128)(2,1)S(1)}, u32[]{:S(2)}, u32[]{:S(2)}) collective-permute-start(bf16[1,9,2048]{2,1,0:T(8,128)(2,1)S(1)} %get-tuple-element.569), channel_id=1, source_target_pairs={{0,4},{1,5},{2,6},{3,7},{4,0},{5,1},{6,2},{7,3},{8,12},{9,13},{10,... | collective-permute-start | bytes 110600 | tf_op jit(solution)/shard_map/while/body/eval_jaxpr/ppermute | solution.py:25
  714.0 17.0 %collective-permute-start.5 = (bf16[1,9,2048]{2,1,0:T(8,128)(2,1)S(1)}, bf16[1,9,2048]{2,1,0:T(8,128)(2,1)S(1)}, u32[]{:S(2)}, u32[]{:S(2)}) collective-permute-start(bf16[1,9,2048]{2,1,0:T(8,128)(2,1)S(1)} %get-tuple-element.570), channel_id=1, source_target_pairs={{0,5},{1,4},{2,7},{3,6},{4,1},{5,0},{6,3},{7,2},{8,13},{9,12},{10,... | collective-permute-start | bytes 110600 | tf_op jit(solution)/shard_map/while/body/eval_jaxpr/ppermute | solution.py:25
  767.6 28.9 %all-to-all-start = ((bf16[8,9,2048]{2,1,0:T(8,128)(2,1)}), bf16[8,9,2048]{2,1,0:T(8,128)(2,1)S(1)}, u32[]{:S(2)}, u32[]{:S(2)}) async-start(bf16[8,9,2048]{2,1,0:T(8,128)(2,1)} %reshape.281), calls=%async_computation | async-start | bytes 1048576 | tf_op jit(solution)/shard_map/while/body/eval_jaxpr/all_to_all | solution.py:143
  776.6 17.5 %collective-permute-start.4 = (bf16[1,9,2048]{2,1,0:T(8,128)(2,1)S(1)}, bf16[1,9,2048]{2,1,0:T(8,128)(2,1)S(1)}, u32[]{:S(2)}, u32[]{:S(2)}) collective-permute-start(bf16[1,9,2048]{2,1,0:T(8,128)(2,1)S(1)} %get-tuple-element.569), channel_id=1, source_target_pairs={{0,4},{1,5},{2,6},{3,7},{4,0},{5,1},{6,2},{7,3},{8,12},{9,13},{10,... | collective-permute-start | bytes 110600 | tf_op jit(solution)/shard_map/while/body/eval_jaxpr/ppermute | solution.py:25
  779.4 17.0 %collective-permute-start.5 = (bf16[1,9,2048]{2,1,0:T(8,128)(2,1)S(1)}, bf16[1,9,2048]{2,1,0:T(8,128)(2,1)S(1)}, u32[]{:S(2)}, u32[]{:S(2)}) collective-permute-start(bf16[1,9,2048]{2,1,0:T(8,128)(2,1)S(1)} %get-tuple-element.570), channel_id=1, source_target_pairs={{0,5},{1,4},{2,7},{3,6},{4,1},{5,0},{6,3},{7,2},{8,13},{9,12},{10,... | collective-permute-start | bytes 110600 | tf_op jit(solution)/shard_map/while/body/eval_jaxpr/ppermute | solution.py:25
  (125 other events, 1519.2 us)
